TPU v7x, 32 devices: a whole 2x2x4 slice. The times are simulated.
32 devices in a mesh: rep: 2 (over y), seq: 4 (over z), head: 4 (over x, core).
Axes of the slice: x: 2, y: 2, z: 4, core: 2. Of those that a mesh axis runs over, the one named last changes fastest.
Arguments:
- queries: bfloat16 [3072, 2560], P(('rep', 'seq'), 'head'), parts along dimension 0, may hold values from -16 to 16
- keys: bfloat16 [3072, 2560], P(('rep', 'seq'), 'head'), parts along dimension 0, may hold values from -6 to 6
- values: bfloat16 [3072, 2560], P(('rep', 'seq'), 'head'), parts along dimension 0, may hold values from -6 to 6
- out_weight: bfloat16 [2560, 5120], P('seq', 'head'), may hold values from -0.3125 to 0.3125
- neighbours: int32 [8, 27], P('rep'), parts along dimension 0, may hold values from -1 to 3, as said below
- clip_ids: int32 [3072], P(('rep', 'seq')), parts along dimension 0, may hold values from 0 to 1
Outputs:
- output: bfloat16 [3072, 5120], P(('rep', 'seq'), 'head'), parts along dimension 0
There are 2 independent parts, one for each index of `rep`. A program takes and returns all parts, laid end to end along the dimension named above; an argument that names none is the same for every part. Nothing has to cross between parts.
Inputs may be any that keep to these rules, and one draw needn't show every extreme that they name: `neighbours`: column 9 (a + 1) + 3 (b + 1) + (c + 1) of row s, for a, b, c each -1, 0 or 1, is either -1 or s + a * 4 * 7 + b * 7 + c; column 13 of row s is s.
All inputs are finite; a program needn't handle non-finite values.
Results may differ from a plain program's by a relative error of at most 0.0058.
Values may be sent and summed in bfloat16 or wider, within the bound.
No kernel may reach another device: no remote copies, remote signals or barrier semaphores. Data moves between devices by JAX's collectives and lax.ppermute only.
A program may use at most 192 MiB of HBM per device.

v0:
```python
import math
import jax
import jax.numpy as jnp
from jax import lax
from jax.sharding import PartitionSpec as P

HD = 128
TGH = 4
TGW = 7


def from_behind(value, axis, by):
    peers = lax.axis_size(axis)
    pairs = [(i, i + by) for i in range(peers) if 0 <= i + by < peers]
    return lax.ppermute(value, axis, pairs)


def attend_head(query_head, key_head, value_head, allowed):
    scores = lax.dot_general(
        query_head, key_head, (((1,), (1,)), ((), ())), preferred_element_type=jnp.float32
    ) * (1.0 / math.sqrt(query_head.shape[1]))
    masked = jnp.where(allowed, scores, -1e30)
    highest = jnp.max(masked, axis=1, keepdims=True)
    raised = jnp.where(allowed, jnp.exp(masked - highest), 0.0)
    summed = jnp.sum(raised, axis=1, keepdims=True)
    weights = (raised / summed).astype(jnp.bfloat16)
    return jnp.dot(weights, value_head, preferred_element_type=jnp.float32).astype(jnp.bfloat16)


def on_device(queries, keys, values, out_weight, neighbours, clip_ids):
    tile_rows = queries.shape[0]
    feature_width = queries.shape[1]
    seq_count = lax.axis_size("seq")
    layer_tiles = TGH * TGW
    every_offset = set()
    for layer_step in (-1, 0, 1):
        for row_step in (-1, 0, 1):
            for col_step in (-1, 0, 1):
                every_offset.add(layer_step * layer_tiles + row_step * TGW + col_step)
    distances = [offset for offset in sorted(every_offset) if 0 < offset < seq_count]
    key_list = [keys]
    value_list = [values]
    clip_list = [clip_ids]
    offsets = [0]
    for distance in distances:
        below_keys, below_values, below_clips = from_behind(
            (keys, values, clip_ids), "seq", distance
        )
        above_keys, above_values, above_clips = from_behind(
            (keys, values, clip_ids), "seq", -distance
        )
        key_list += [below_keys, above_keys]
        value_list += [below_values, above_values]
        clip_list += [below_clips, above_clips]
        offsets += [distance, -distance]
    key_stack = jnp.stack(key_list)
    value_stack = jnp.stack(value_list)
    clip_stack = jnp.stack(clip_list)
    blocks = key_stack.shape[0]
    position = lax.axis_index("seq")
    window_row = lax.dynamic_index_in_dim(neighbours, position, 0, keepdims=False)
    sources = position - jnp.asarray(offsets, dtype=jnp.int32)
    present = jnp.any(
        (window_row[None, :] == sources[:, None]) & (window_row[None, :] >= 0), axis=1
    )
    key_clips = clip_stack.reshape(blocks * tile_rows)
    allowed = jnp.repeat(present, tile_rows)[None, :] & (clip_ids[:, None] == key_clips[None, :])
    key_rows = key_stack.reshape(blocks * tile_rows, feature_width)
    value_rows = value_stack.reshape(blocks * tile_rows, feature_width)
    head_outputs = []
    for head_index in range(feature_width // HD):
        first_col = head_index * HD
        head_outputs.append(
            attend_head(
                queries[:, first_col : first_col + HD],
                key_rows[:, first_col : first_col + HD],
                value_rows[:, first_col : first_col + HD],
                allowed,
            )
        )
    attended = jnp.concatenate(head_outputs, axis=1)
    all_features = lax.all_gather(attended, "head", axis=1, tiled=True)
    empty = jnp.zeros((tile_rows, out_weight.shape[1]), jnp.float32)
    weight_piece = lax.all_gather(out_weight, "seq", axis=0, tiled=True)
    features = lax.slice_in_dim(all_features, 0, weight_piece.shape[0], axis=1)
    projected = empty + jnp.dot(features, weight_piece, preferred_element_type=jnp.float32)
    return projected.astype(jnp.bfloat16)


def solution(mesh):
    in_specs = (
        P(("rep", "seq"), "head"),
        P(("rep", "seq"), "head"),
        P(("rep", "seq"), "head"),
        P("seq", "head"),
        P("rep", None),
        P(("rep", "seq")),
    )
    out_specs = P(("rep", "seq"), "head")
    return jax.shard_map(
        on_device, mesh=mesh, in_specs=in_specs, out_specs=out_specs, check_vma=False
    )
```

profile of v0, /device:TPU:0, one launch (start us, length us, event | category | flops | bytes accessed | tf_op | source)
XLA Modules:
  0.0 208.0 jit_solution(14518805611755408136)
XLA Ops:
  6.5 5.0 %collective-permute-start = (s32[384]{0:T(512)}, s32[384]{0:T(512)S(1)}, u32[]{:S(2)}, u32[]{:S(2)}) collective-permute-start(s32[384]{0:T(512)} %param.12), channel_id=1, source_target_pairs={{0,4},{4,8},{8,12},{1,5},{5,9},{9,13},{2,6},{6,10},{10,14},{3,7},{... | collective-permute-start | bytes 4616 | tf_op jit(solution)/shard_map/ppermute | solution.py:15
  11.6 1.3 collective-permute-start.1
  12.9 4.6 %collective-permute-start.2 = (bf16[384,640]{1,0:T(8,128)(2,1)}, bf16[384,640]{1,0:T(8,128)(2,1)S(1)}, u32[]{:S(2)}, u32[]{:S(2)}) collective-permute-start(bf16[384,640]{1,0:T(8,128)(2,1)} %param.8), channel_id=1, source_target_pairs={{0,4},{4,8},{8,12},{1,5},{5,9},{9,13},{2,6},{6,10},{10,14},{3,7},{... | collective-permute-start | bytes 1474568 | tf_op jit(solution)/shard_map/ppermute | solution.py:15
  17.5 1.3 collective-permute-start.3
  18.8 4.6 %collective-permute-start.4 = (bf16[384,640]{1,0:T(8,128)(2,1)}, bf16[384,640]{1,0:T(8,128)(2,1)S(1)}, u32[]{:S(2)}, u32[]{:S(2)}) collective-permute-start(bf16[384,640]{1,0:T(8,128)(2,1)} %param.9), channel_id=1, source_target_pairs={{0,4},{4,8},{8,12},{1,5},{5,9},{9,13},{2,6},{6,10},{10,14},{3,7},{... | collective-permute-start | bytes 1474568 | tf_op jit(solution)/shard_map/ppermute | solution.py:15
  23.4 0.7 compare_bitcast_fusion
  24.1 0.7 fusion.35
  24.8 0.7 broadcast_add_fusion
  25.4 0.2 and_reduce_fusion
  25.6 0.7 stack.36
  26.4 1.3 collective-permute-start.5
  27.8 1.7 collective-permute-done.2
  29.4 4.3 %collective-permute-done.3 = bf16[384,640]{1,0:T(8,128)(2,1)S(1)} collective-permute-done((bf16[384,640]{1,0:T(8,128)(2,1)}, bf16[384,640]{1,0:T(8,128)(2,1)S(1)}, u32[]{:S(2)}, u32[]{:S(2)}) %collective-permute-start.3) | collective-permute-done | bytes 491552 | tf_op jit(solution)/shard_map/ppermute | solution.py:15
  33.8 1.2 pad_maximum_fusion
  35.0 0.6 fusion.41
  35.6 0.6 fusion.42
  36.3 0.6 fusion.43
  36.9 0.6 fusion.44
  37.5 0.6 fusion.45
  38.2 4.0 %collective-permute-done.5 = bf16[384,640]{1,0:T(8,128)(2,1)S(1)} collective-permute-done((bf16[384,640]{1,0:T(8,128)(2,1)}, bf16[384,640]{1,0:T(8,128)(2,1)S(1)}, u32[]{:S(2)}, u32[]{:S(2)}) %collective-permute-start.5) | collective-permute-done | bytes 491552 | tf_op jit(solution)/shard_map/ppermute | solution.py:15
  42.3 0.2 pad_maximum_fusion.1
  42.4 2.3 %fusion.14 = (f32[384]{0:T(512)S(1)}, f32[384]{0:T(512)S(1)}, f32[384]{0:T(512)S(1)}, f32[384]{0:T(512)S(1)}, f32[384]{0:T(512)S(1)}) fusion(f32[384,1152]{0,1:T(8,128)S(1)} %get-tuple-element.11, f32[384]{0:T(512)S(1)} %get-tuple-element.10, s32[384]{0:T(512)S(1)} %copy-done.2, s32[1152]{0:T(1024)S(1)} %eq.35, pred[1152]{0:T(1024)(128)(4,1)S(1)} %and.24, ...), kind=kLoop, calls=%fused_computation.33 | loop fusion | flops 7518336 | bytes 8870016 | tf_op jit(solution)/shard_map/reduce_sum | solution.py:25
  44.7 1.0 fusion.15
  45.7 1.0 fusion.16
  46.8 1.0 fusion.17
  47.8 1.0 fusion.18
  48.8 1.0 fusion.19
  49.8 0.8 copy-done.1
  50.7 0.7 all-gather.5.cloned.1.call-update
  51.4 21.5 %all-gather.3.cloned.1.call-done = bf16[384,2560]{1,0:T(8,128)(2,1)} async-done(((bf16[384,640]{1,0:T(8,128)(2,1)}), bf16[384,2560]{1,0:T(8,128)(2,1)}) %all-gather.3.cloned.1.call-update) | async-done | bytes 1966096 | tf_op jit(solution)/shard_map/all_gather | solution.py:82
  72.8 121.2 %all-gather.5.cloned.1.call-done = bf16[2560,1280]{1,0:T(8,128)(2,1)} async-done(((bf16[640,1280]{1,0:T(8,128)(2,1)}), bf16[2560,1280]{1,0:T(8,128)(2,1)}) %all-gather.5.cloned.1.call-update) | async-done | bytes 6553616 | tf_op jit(solution)/shard_map/all_gather | solution.py:84
  194.1 7.1 %convolution_convert_fusion = bf16[384,1280]{1,0:T(8,128)(2,1)} fusion(bf16[384,2560]{1,0:T(8,128)(2,1)} %all-gather.3.cloned.1.call-done, bf16[2560,1280]{1,0:T(8,128)(2,1)} %all-gather.5.cloned.1.call-done), kind=kOutput, calls=%fused_computation.15 | convolution fusion | flops 2517073920 | bytes 9502720 | tf_op jit(solution)/shard_map/dot_general | solution.py:86
  (19 shorter events, 0.3 us)
Async XLA Ops:
  6.5 28.4 %copy-start.2 = (s32[384]{0:T(512)S(1)}, s32[384]{0:T(512)}, u32[]{:S(2)}) copy-start(s32[384]{0:T(512)} %param.12) | copy-start | bytes 4612
  6.5 28.5 %copy-start.3 = (bf16[384,640]{1,0:T(8,128)(2,1)S(1)}, bf16[384,640]{1,0:T(8,128)(2,1)}, u32[]{:S(2)}) copy-start(bf16[384,640]{1,0:T(8,128)(2,1)} %param.7) | copy-start | bytes 1474564
  6.5 66.3 %all-gather.3.cloned.1.call-start = ((), (), s32[]{:S(2)}) async-start(), calls=%async_computation | async-start | bytes 2457600 | tf_op jit(solution)/shard_map/all_gather | solution.py:82
  6.5 19.8 %collective-permute-start = (s32[384]{0:T(512)}, s32[384]{0:T(512)S(1)}, u32[]{:S(2)}, u32[]{:S(2)}) collective-permute-start(s32[384]{0:T(512)} %param.12), channel_id=1, source_target_pairs={{0,4},{4,8},{8,12},{1,5},{5,9},{9,13},{2,6},{6,10},{10,14},{3,7},{... | collective-permute-start | bytes 4616 | tf_op jit(solution)/shard_map/ppermute | solution.py:15
  11.6 16.1 %collective-permute-start.1 = (s32[384]{0:T(512)}, s32[384]{0:T(512)S(1)}, u32[]{:S(2)}, u32[]{:S(2)}) collective-permute-start(s32[384]{0:T(512)} %param.12), channel_id=1, source_target_pairs={{4,0},{8,4},{12,8},{5,1},{9,5},{13,9},{6,2},{10,6},{14,10},{7,3},{... | collective-permute-start | bytes 4616 | tf_op jit(solution)/shard_map/ppermute | solution.py:15
  12.9 16.5 %collective-permute-start.2 = (bf16[384,640]{1,0:T(8,128)(2,1)}, bf16[384,640]{1,0:T(8,128)(2,1)S(1)}, u32[]{:S(2)}, u32[]{:S(2)}) collective-permute-start(bf16[384,640]{1,0:T(8,128)(2,1)} %param.8), channel_id=1, source_target_pairs={{0,4},{4,8},{8,12},{1,5},{5,9},{9,13},{2,6},{6,10},{10,14},{3,7},{... | collective-permute-start | bytes 1474568 | tf_op jit(solution)/shard_map/ppermute | solution.py:15
  17.5 16.3 %collective-permute-start.3 = (bf16[384,640]{1,0:T(8,128)(2,1)}, bf16[384,640]{1,0:T(8,128)(2,1)S(1)}, u32[]{:S(2)}, u32[]{:S(2)}) collective-permute-start(bf16[384,640]{1,0:T(8,128)(2,1)} %param.8), channel_id=1, source_target_pairs={{4,0},{8,4},{12,8},{5,1},{9,5},{13,9},{6,2},{10,6},{14,10},{7,3},{... | collective-permute-start | bytes 1474568 | tf_op jit(solution)/shard_map/ppermute | solution.py:15
  18.8 19.4 %collective-permute-start.4 = (bf16[384,640]{1,0:T(8,128)(2,1)}, bf16[384,640]{1,0:T(8,128)(2,1)S(1)}, u32[]{:S(2)}, u32[]{:S(2)}) collective-permute-start(bf16[384,640]{1,0:T(8,128)(2,1)} %param.9), channel_id=1, source_target_pairs={{0,4},{4,8},{8,12},{1,5},{5,9},{9,13},{2,6},{6,10},{10,14},{3,7},{... | collective-permute-start | bytes 1474568 | tf_op jit(solution)/shard_map/ppermute | solution.py:15
  26.4 15.9 %collective-permute-start.5 = (bf16[384,640]{1,0:T(8,128)(2,1)}, bf16[384,640]{1,0:T(8,128)(2,1)S(1)}, u32[]{:S(2)}, u32[]{:S(2)}) collective-permute-start(bf16[384,640]{1,0:T(8,128)(2,1)} %param.9), channel_id=1, source_target_pairs={{4,0},{8,4},{12,8},{5,1},{9,5},{13,9},{6,2},{10,6},{14,10},{7,3},{... | collective-permute-start | bytes 1474568 | tf_op jit(solution)/shard_map/ppermute | solution.py:15
  37.5 4.7 %copy-start = (bf16[384,640]{1,0:T(8,128)(2,1)S(1)}, bf16[384,640]{1,0:T(8,128)(2,1)}, u32[]{:S(2)}) copy-start(bf16[384,640]{1,0:T(8,128)(2,1)} %param.9) | copy-start | bytes 1474564
  49.8 0.8 copy-start.1
  50.6 143.4 %all-gather.5.cloned.1.call-start = ((), (), s32[]{:S(2)}) async-start(), calls=%async_computation.1 | async-start | bytes 8192000 | tf_op jit(solution)/shard_map/all_gather | solution.py:84
Sparse Core Ops, SparseCore 0:
  50.7 22.0 all-gather.2
  74.4 119.6 all-gather.4
where the time goes:
time: 208 us
  waiting for transfers between devices  154 us (74%)
  starting transfers between devices  18.1 us (9%)
  matrix products  15.3 us (7%)
  between operations  13.6 us (7%)
  other arithmetic  5.25 us (3%)
  local copies, waits for them, and re-layouts  2.27 us (1%)
    all_gather x1, waiting for transfers between devices, on_device(): weight_piece = lax.all_gather(out_weight, 'seq', axis=0, tiled=True)  121 us
    all_gather x1, waiting for transfers between devices, on_device(): all_features = lax.all_gather(attended, 'head', axis=1, tiled=True)  21.5 us
    ppermute x6, starting transfers between devices, from_behind(): return lax.ppermute(value, axis, pairs)  18.1 us
    ppermute x6, waiting for transfers between devices, from_behind(): return lax.ppermute(value, axis, pairs)  10.1 us
    dot_general x1, matrix products, on_device(): jnp.dot(features, weight_piece, preferred_element_type=jnp.float32)  7.1 us
    dot_general x5, matrix products, attend_head(): jnp.dot(weights, value_head, preferred_element_type=jnp.float32)  5.04 us
  transfers between devices with their start and end apart: 8, of which 6 were waited for; matrix products, arithmetic and copies ran while one was open for 4% of the time, Pallas kernels for 0%

commit v1 on v0

--- a/solution.py
+++ b/solution.py
@@ -81,7 +81,22 @@
     attended = jnp.concatenate(head_outputs, axis=1)
     all_features = lax.all_gather(attended, "head", axis=1, tiled=True)
     empty = jnp.zeros((tile_rows, out_weight.shape[1]), jnp.float32)
-    weight_piece = lax.all_gather(out_weight, "seq", axis=0, tiled=True)
+    ways, here, step = (lax.axis_size("seq"), lax.axis_index("seq"), out_weight.shape[0])
+    shape = [n * ways if d == 0 else n for d, n in enumerate(out_weight.shape)]
+    weight_piece = lax.dynamic_update_slice_in_dim(
+        jnp.zeros(shape, out_weight.dtype), out_weight, here * step, axis=0
+    )
+    going_up = going_down = out_weight
+    for far in range(1, ways // 2 + 1):
+        going_up = lax.ppermute(going_up, "seq", [(d, (d + 1) % ways) for d in range(ways)])
+        weight_piece = lax.dynamic_update_slice_in_dim(
+            weight_piece, going_up, (here - far) % ways * step, axis=0
+        )
+        if 2 * far < ways:
+            going_down = lax.ppermute(going_down, "seq", [(d, (d - 1) % ways) for d in range(ways)])
+            weight_piece = lax.dynamic_update_slice_in_dim(
+                weight_piece, going_down, (here + far) % ways * step, axis=0
+            )
     features = lax.slice_in_dim(all_features, 0, weight_piece.shape[0], axis=1)
     projected = empty + jnp.dot(features, weight_piece, preferred_element_type=jnp.float32)
     return projected.astype(jnp.bfloat16)

time: 208 us -> 167 us (0.80)
  waiting for transfers between devices: 154 us -> 91 us
  local copies, waits for them, and re-layouts: 2.27 us -> 12.7 us
  starting transfers between devices: 18.1 us -> 24.4 us
  matrix products: 15.3 us -> 18.5 us
    all_gather x1 -> x0, waiting for transfers between devices: 121 us -> none  [on_device(): weight_piece = lax.all_gather(out_weight, 'seq', axis=0, tiled=True)]
    ppermute x0 -> x3, waiting for transfers between devices: none -> 83.5 us  [the longest x2 54.1 us: on_device(): lax.ppermute(going_up, 'seq', [(d, (d + 1) % ways) for d in range(ways)])]
    all_gather x1, waiting for transfers between devices: 21.5 us -> 0.01 us  [on_device(): all_features = lax.all_gather(attended, 'head', axis=1, tiled=True)]
    dynamic_update_slice x0 -> x4, local copies, waits for them, and re-layouts: none -> 8.02 us  [the longest x2 4.01 us: on_device(): lax.dynamic_update_slice_in_dim(weight_piece, going_up, (here - far) % wa...]
    ppermute x0 -> x3, starting transfers between devices: none -> 6.3 us  [the longest x1 3.6 us: on_device(): lax.ppermute(going_down, 'seq', [(d, (d - 1) % ways) for d in range(ways)])]
    dot_general x5, matrix products: 5.04 us -> 8.21 us  [attend_head(): jnp.dot(weights, value_head, preferred_element_type=jnp.float32)]
    broadcast_in_dim x0 -> x1, local copies, waits for them, and re-layouts: none -> 3.16 us  [on_device(): jnp.zeros(shape, out_weight.dtype)]
    ppermute x6, waiting for transfers between devices: 10.1 us -> 7.52 us  [from_behind(): return lax.ppermute(value, axis, pairs)]
  transfers between devices with their start and end apart: 8 -> 10, of which waited for: 6 -> 6; matrix products, arithmetic and copies ran while one was open for 4% -> 18% of each run, Pallas kernels for 0% -> 0%
where the time goes in v1:
time: 167 us; the launch traced here: 166 us
  waiting for transfers between devices  91 us (54%)
  starting transfers between devices  24.4 us (15%)
  matrix products  18.5 us (11%)
  between operations  13.5 us (8%)
  local copies, waits for them, and re-layouts  12.7 us (8%)
  other arithmetic  6.31 us (4%)
    ppermute x2, waiting for transfers between devices, on_device(): lax.ppermute(going_up, 'seq', [(d, (d + 1) % ways) for d in range(ways)])  54.1 us
    ppermute x1, waiting for transfers between devices, on_device(): lax.ppermute(going_down, 'seq', [(d, (d - 1) % ways) for d in range(ways)])  29.4 us
    ppermute x6, starting transfers between devices, from_behind(): return lax.ppermute(value, axis, pairs)  18.1 us
    dot_general x5, matrix products, attend_head(): jnp.dot(weights, value_head, preferred_element_type=jnp.float32)  8.21 us
    ppermute x6, waiting for transfers between devices, from_behind(): return lax.ppermute(value, axis, pairs)  7.52 us
    dot_general x1, matrix products, on_device(): jnp.dot(features, weight_piece, preferred_element_type=jnp.float32)  7.1 us
    dynamic_update_slice x2, local copies, waits for them, and re-layouts, on_device(): lax.dynamic_update_slice_in_dim(weight_piece, going_up, (here - far) % wa...  4.01 us
    ppermute x1, starting transfers between devices, on_device(): lax.ppermute(going_down, 'seq', [(d, (d - 1) % ways) for d in range(ways)])  3.6 us
  transfers between devices with their start and end apart: 10, of which 6 were waited for; matrix products, arithmetic and copies ran while one was open for 18% of the time, Pallas kernels for 0%

profile of v1, /device:TPU:0, one launch (start us, length us, event | category | flops | bytes accessed | tf_op | source)
XLA Modules:
  0.0 166.4 jit_solution(18132266874616502192)
XLA Ops:
  6.5 5.0 %collective-permute-start = (s32[384]{0:T(512)}, s32[384]{0:T(512)S(1)}, u32[]{:S(2)}, u32[]{:S(2)}) collective-permute-start(s32[384]{0:T(512)} %param.12), channel_id=1, source_target_pairs={{0,4},{4,8},{8,12},{1,5},{5,9},{9,13},{2,6},{6,10},{10,14},{3,7},{... | collective-permute-start | bytes 4616 | tf_op jit(solution)/shard_map/ppermute | solution.py:15
  11.6 1.3 collective-permute-start.1
  12.9 4.6 %collective-permute-start.2 = (bf16[384,640]{1,0:T(8,128)(2,1)}, bf16[384,640]{1,0:T(8,128)(2,1)S(1)}, u32[]{:S(2)}, u32[]{:S(2)}) collective-permute-start(bf16[384,640]{1,0:T(8,128)(2,1)} %param.8), channel_id=1, source_target_pairs={{0,4},{4,8},{8,12},{1,5},{5,9},{9,13},{2,6},{6,10},{10,14},{3,7},{... | collective-permute-start | bytes 1474568 | tf_op jit(solution)/shard_map/ppermute | solution.py:15
  17.5 1.3 collective-permute-start.3
  18.8 4.6 %collective-permute-start.4 = (bf16[384,640]{1,0:T(8,128)(2,1)}, bf16[384,640]{1,0:T(8,128)(2,1)S(1)}, u32[]{:S(2)}, u32[]{:S(2)}) collective-permute-start(bf16[384,640]{1,0:T(8,128)(2,1)} %param.9), channel_id=1, source_target_pairs={{0,4},{4,8},{8,12},{1,5},{5,9},{9,13},{2,6},{6,10},{10,14},{3,7},{... | collective-permute-start | bytes 1474568 | tf_op jit(solution)/shard_map/ppermute | solution.py:15
  23.4 0.7 compare_bitcast_fusion
  24.1 0.7 fusion.35
  24.8 0.7 broadcast_add_fusion
  25.6 0.7 stack.36
  26.4 1.3 collective-permute-start.5
  27.7 2.7 %collective-permute-start.6 = (bf16[640,1280]{1,0:T(8,128)(2,1)}, bf16[640,1280]{1,0:T(8,128)(2,1)S(1)}, u32[]{:S(2)}, u32[]{:S(2)}) collective-permute-start(bf16[640,1280]{1,0:T(8,128)(2,1)} %param.10), channel_id=1, source_target_pairs={{0,4},{4,8},{8,12},{12,0},{1,5},{5,9},{9,13},{13,1},{2,6},{6,10},{... | collective-permute-start | bytes 4915208 | tf_op jit(solution)/shard_map/ppermute | solution.py:91
  30.5 3.3 %collective-permute-done.3 = bf16[384,640]{1,0:T(8,128)(2,1)S(1)} collective-permute-done((bf16[384,640]{1,0:T(8,128)(2,1)}, bf16[384,640]{1,0:T(8,128)(2,1)S(1)}, u32[]{:S(2)}, u32[]{:S(2)}) %collective-permute-start.3) | collective-permute-done | bytes 491552 | tf_op jit(solution)/shard_map/ppermute | solution.py:15
  33.8 1.2 pad_maximum_fusion
  38.2 1.8 %collective-permute-done.4 = bf16[384,640]{1,0:T(8,128)(2,1)S(1)} collective-permute-done((bf16[384,640]{1,0:T(8,128)(2,1)}, bf16[384,640]{1,0:T(8,128)(2,1)S(1)}, u32[]{:S(2)}, u32[]{:S(2)}) %collective-permute-start.4) | collective-permute-done | bytes 491552 | tf_op jit(solution)/shard_map/ppermute | solution.py:15
  40.0 2.4 %collective-permute-done.5 = bf16[384,640]{1,0:T(8,128)(2,1)} collective-permute-done((bf16[384,640]{1,0:T(8,128)(2,1)}, bf16[384,640]{1,0:T(8,128)(2,1)}, u32[]{:S(2)}, u32[]{:S(2)}) %collective-permute-start.5) | collective-permute-done | bytes 491552 | tf_op jit(solution)/shard_map/ppermute | solution.py:15
  42.4 1.2 pad_maximum_fusion.1
  43.6 2.3 %fusion.14 = (f32[384]{0:T(512)S(1)}, f32[384]{0:T(512)S(1)}, f32[384]{0:T(512)S(1)}, f32[384]{0:T(512)S(1)}, f32[384]{0:T(512)S(1)}) fusion(f32[384,1152]{0,1:T(8,128)S(1)} %get-tuple-element.11, f32[384]{0:T(512)S(1)} %get-tuple-element.10, s32[384]{0:T(512)S(1)} %copy-done.2, s32[1152]{0:T(1024)S(1)} %eq.39, pred[1152]{0:T(1024)(128)(4,1)S(1)} %and.37, ...), kind=kLoop, calls=%fused_computation.33 | loop fusion | flops 7518336 | bytes 8870016 | tf_op jit(solution)/shard_map/reduce_sum | solution.py:25
  45.9 1.6 fusion.15
  47.6 1.6 fusion.16
  49.2 1.6 fusion.17
  50.9 1.6 fusion.18
  52.5 1.6 fusion.19
  54.2 3.6 %collective-permute-start.7 = (bf16[640,1280]{1,0:T(8,128)(2,1)S(1)}, bf16[640,1280]{1,0:T(8,128)(2,1)}, u32[]{:S(2)}, u32[]{:S(2)}) collective-permute-start(bf16[640,1280]{1,0:T(8,128)(2,1)S(1)} %copy-done), channel_id=1, source_target_pairs={{0,12},{4,0},{8,4},{12,8},{1,13},{5,1},{9,5},{13,9},{2,14},{6,2},{... | collective-permute-start | bytes 4915208 | tf_op jit(solution)/shard_map/ppermute | solution.py:96
  57.8 23.6 %collective-permute-done.6 = bf16[640,1280]{1,0:T(8,128)(2,1)S(1)} collective-permute-done((bf16[640,1280]{1,0:T(8,128)(2,1)}, bf16[640,1280]{1,0:T(8,128)(2,1)S(1)}, u32[]{:S(2)}, u32[]{:S(2)}) %collective-permute-start.6) | collective-permute-done | bytes 1638432 | tf_op jit(solution)/shard_map/ppermute | solution.py:91
  81.4 3.2 %broadcast_in_dim.38 = bf16[2560,1280]{1,0:T(8,128)(2,1)} broadcast(bf16[]{:T(256)} %constant.50.clone.1), dimensions={} | broadcast | bytes 6553602 | tf_op jit(solution)/shard_map/broadcast_in_dim | solution.py:87
  84.6 1.3 constant_dynamic-update-slice_fusion.3
  85.9 1.3 constant_dynamic-update-slice_fusion.2
  87.2 29.4 %collective-permute-done.7 = bf16[640,1280]{1,0:T(8,128)(2,1)} collective-permute-done((bf16[640,1280]{1,0:T(8,128)(2,1)S(1)}, bf16[640,1280]{1,0:T(8,128)(2,1)}, u32[]{:S(2)}, u32[]{:S(2)}) %collective-permute-start.7) | collective-permute-done | bytes 1638432 | tf_op jit(solution)/shard_map/ppermute | solution.py:96
  116.6 2.7 %constant_dynamic-update-slice_fusion.1 = bf16[2560,1280]{1,0:T(8,128)(2,1)} fusion(bf16[2560,1280]{1,0:T(8,128)(2,1)} %constant_dynamic-update-slice_fusion.2, bf16[640,1280]{1,0:T(8,128)(2,1)} %collective-permute-done.7, s32[]{:T(128)S(6)} %select_n.77), kind=kLoop, calls=%fused_computation.63 | loop fusion | bytes 3276804 | tf_op jit(solution)/shard_map/dynamic_update_slice | solution.py:97
  119.3 30.4 %collective-permute-done.8 = bf16[640,1280]{1,0:T(8,128)(2,1)} collective-permute-done((bf16[640,1280]{1,0:T(8,128)(2,1)S(1)}, bf16[640,1280]{1,0:T(8,128)(2,1)}, u32[]{:S(2)}, u32[]{:S(2)}) %collective-permute-start.8) | collective-permute-done | bytes 1638432 | tf_op jit(solution)/shard_map/ppermute | solution.py:91
  149.7 2.7 %constant_dynamic-update-slice_fusion = bf16[2560,1280]{1,0:T(8,128)(2,1)} fusion(bf16[2560,1280]{1,0:T(8,128)(2,1)} %constant_dynamic-update-slice_fusion.1, bf16[640,1280]{1,0:T(8,128)(2,1)} %collective-permute-done.8, s32[]{:T(128)S(6)} %select_n.79), kind=kLoop, calls=%fused_computation.62 | loop fusion | bytes 3276804 | tf_op jit(solution)/shard_map/dynamic_update_slice | solution.py:92
  152.4 7.1 %convolution_convert_fusion = bf16[384,1280]{1,0:T(8,128)(2,1)} fusion(bf16[384,2560]{1,0:T(8,128)(2,1)} %all-gather.2.cloned.1.call-done, bf16[2560,1280]{1,0:T(8,128)(2,1)} %constant_dynamic-update-slice_fusion), kind=kOutput, calls=%fused_computation.15 | convolution fusion | flops 2517073920 | bytes 9502720 | tf_op jit(solution)/shard_map/dot_general | solution.py:101
  (27 shorter events, 3.5 us)
Async XLA Ops:
  6.5 28.4 %copy-start.2 = (s32[384]{0:T(512)S(1)}, s32[384]{0:T(512)}, u32[]{:S(2)}) copy-start(s32[384]{0:T(512)} %param.12) | copy-start | bytes 4612
  6.5 145.9 %all-gather.2.cloned.1.call-start = ((), (), s32[]{:S(2)}) async-start(), calls=%async_computation | async-start | bytes 2457600 | tf_op jit(solution)/shard_map/all_gather | solution.py:82
  6.5 19.8 %collective-permute-start = (s32[384]{0:T(512)}, s32[384]{0:T(512)S(1)}, u32[]{:S(2)}, u32[]{:S(2)}) collective-permute-start(s32[384]{0:T(512)} %param.12), channel_id=1, source_target_pairs={{0,4},{4,8},{8,12},{1,5},{5,9},{9,13},{2,6},{6,10},{10,14},{3,7},{... | collective-permute-start | bytes 4616 | tf_op jit(solution)/shard_map/ppermute | solution.py:15
  11.6 16.1 %collective-permute-start.1 = (s32[384]{0:T(512)}, s32[384]{0:T(512)S(1)}, u32[]{:S(2)}, u32[]{:S(2)}) collective-permute-start(s32[384]{0:T(512)} %param.12), channel_id=1, source_target_pairs={{4,0},{8,4},{12,8},{5,1},{9,5},{13,9},{6,2},{10,6},{14,10},{7,3},{... | collective-permute-start | bytes 4616 | tf_op jit(solution)/shard_map/ppermute | solution.py:15
  12.9 17.6 %collective-permute-start.2 = (bf16[384,640]{1,0:T(8,128)(2,1)}, bf16[384,640]{1,0:T(8,128)(2,1)S(1)}, u32[]{:S(2)}, u32[]{:S(2)}) collective-permute-start(bf16[384,640]{1,0:T(8,128)(2,1)} %param.8), channel_id=1, source_target_pairs={{0,4},{4,8},{8,12},{1,5},{5,9},{9,13},{2,6},{6,10},{10,14},{3,7},{... | collective-permute-start | bytes 1474568 | tf_op jit(solution)/shard_map/ppermute | solution.py:15
  17.5 16.3 %collective-permute-start.3 = (bf16[384,640]{1,0:T(8,128)(2,1)}, bf16[384,640]{1,0:T(8,128)(2,1)S(1)}, u32[]{:S(2)}, u32[]{:S(2)}) collective-permute-start(bf16[384,640]{1,0:T(8,128)(2,1)} %param.8), channel_id=1, source_target_pairs={{4,0},{8,4},{12,8},{5,1},{9,5},{13,9},{6,2},{10,6},{14,10},{7,3},{... | collective-permute-start | bytes 1474568 | tf_op jit(solution)/shard_map/ppermute | solution.py:15
  18.8 21.2 %collective-permute-start.4 = (bf16[384,640]{1,0:T(8,128)(2,1)}, bf16[384,640]{1,0:T(8,128)(2,1)S(1)}, u32[]{:S(2)}, u32[]{:S(2)}) collective-permute-start(bf16[384,640]{1,0:T(8,128)(2,1)} %param.9), channel_id=1, source_target_pairs={{0,4},{4,8},{8,12},{1,5},{5,9},{9,13},{2,6},{6,10},{10,14},{3,7},{... | collective-permute-start | bytes 1474568 | tf_op jit(solution)/shard_map/ppermute | solution.py:15
  26.4 16.0 %collective-permute-start.5 = (bf16[384,640]{1,0:T(8,128)(2,1)}, bf16[384,640]{1,0:T(8,128)(2,1)}, u32[]{:S(2)}, u32[]{:S(2)}) collective-permute-start(bf16[384,640]{1,0:T(8,128)(2,1)} %param.9), channel_id=1, source_target_pairs={{4,0},{8,4},{12,8},{5,1},{9,5},{13,9},{6,2},{10,6},{14,10},{7,3},{... | collective-permute-start | bytes 1474568 | tf_op jit(solution)/shard_map/ppermute | solution.py:15
  27.7 53.7 %collective-permute-start.6 = (bf16[640,1280]{1,0:T(8,128)(2,1)}, bf16[640,1280]{1,0:T(8,128)(2,1)S(1)}, u32[]{:S(2)}, u32[]{:S(2)}) collective-permute-start(bf16[640,1280]{1,0:T(8,128)(2,1)} %param.10), channel_id=1, source_target_pairs={{0,4},{4,8},{8,12},{12,0},{1,5},{5,9},{9,13},{13,1},{2,6},{6,10},{... | collective-permute-start | bytes 4915208 | tf_op jit(solution)/shard_map/ppermute | solution.py:91
  30.4 4.6 %copy-start.3 = (bf16[384,640]{1,0:T(8,128)(2,1)S(1)}, bf16[384,640]{1,0:T(8,128)(2,1)}, u32[]{:S(2)}) copy-start(bf16[384,640]{1,0:T(8,128)(2,1)} %param.7) | copy-start | bytes 1474564
  37.5 4.9 %copy-start.1 = (bf16[384,640]{1,0:T(8,128)(2,1)S(1)}, bf16[384,640]{1,0:T(8,128)(2,1)}, u32[]{:S(2)}) copy-start(bf16[384,640]{1,0:T(8,128)(2,1)} %param.9) | copy-start | bytes 1474564
  52.5 1.7 %copy-start = (bf16[640,1280]{1,0:T(8,128)(2,1)S(1)}, bf16[640,1280]{1,0:T(8,128)(2,1)}, u32[]{:S(2)}) copy-start(bf16[640,1280]{1,0:T(8,128)(2,1)} %param.10) | copy-start | bytes 4915204
  54.2 62.4 %collective-permute-start.7 = (bf16[640,1280]{1,0:T(8,128)(2,1)S(1)}, bf16[640,1280]{1,0:T(8,128)(2,1)}, u32[]{:S(2)}, u32[]{:S(2)}) collective-permute-start(bf16[640,1280]{1,0:T(8,128)(2,1)S(1)} %copy-done), channel_id=1, source_target_pairs={{0,12},{4,0},{8,4},{12,8},{1,13},{5,1},{9,5},{13,9},{2,14},{6,2},{... | collective-permute-start | bytes 4915208 | tf_op jit(solution)/shard_map/ppermute | solution.py:96
  81.4 68.3 %collective-permute-start.8 = (bf16[640,1280]{1,0:T(8,128)(2,1)S(1)}, bf16[640,1280]{1,0:T(8,128)(2,1)}, u32[]{:S(2)}, u32[]{:S(2)}) collective-permute-start(bf16[640,1280]{1,0:T(8,128)(2,1)S(1)} %collective-permute-done.6), channel_id=1, source_target_pairs={{0,4},{4,8},{8,12},{12,0},{1,5},{5,9},{9,13},{13,1},{2,6},{6,10},{... | collective-permute-start | bytes 4915208 | tf_op jit(solution)/shard_map/ppermute | solution.py:91
Sparse Core Ops, SparseCore 0:
  54.3 24.0 all-gather.1
